TPU v7x, 256 devices: a whole 4x4x8 slice. The times are simulated.
256 devices in a mesh: seq: 32 (over x_hi, z, core), tensor: 8 (over y, x_lo).
Axes of the slice: x: 4 (x_hi: 2, x_lo: 2; x = x_hi * 2 + x_lo), y: 4, z: 8, core: 2. Of those that a mesh axis runs over, the one named last changes fastest.
Arguments:
- tokens: bfloat16 [4, 1024, 4096], P(None, 'seq', 'tensor'), may hold values from -600 to 600
- norm_gain: bfloat16 [4096], replicated, may hold values from 0.099609375 to 1.8984375
- w_query: bfloat16 [4096, 2048], P(None, 'tensor'), may hold values from -0.1875 to 0.1875
- w_key: bfloat16 [4096, 2048], P(None, 'tensor'), may hold values from -0.09375 to 0.09375
- w_value: bfloat16 [4096, 2048], P(None, 'tensor'), may hold values from -0.09375 to 0.09375
- w_out: bfloat16 [2048, 4096], P('tensor'), may hold values from -1 to 1
- cache_keys: bfloat16 [4, 8192, 2048], P(None, 'seq', 'tensor'), may hold values from -103 to 103
- cache_values: bfloat16 [4, 8192, 2048], P(None, 'seq', 'tensor'), may hold values from -6 to 6
- cache_len: int32 [4], replicated, may hold values from 1 to 8192, as said below
- group_len: int32 [4], replicated, may hold values from 1 to 1024, 3584 in all
Outputs:
- mixed: bfloat16 [4, 1024, 4096], P(None, 'seq', 'tensor')
- new_keys: bfloat16 [4, 1024, 2048], P(None, 'seq', 'tensor')
- new_values: bfloat16 [4, 1024, 2048], P(None, 'seq', 'tensor')
Inputs may be any that keep to these rules, and one draw needn't show every extreme that they name: `cache_len`: one request's cache holds all 8192 positions. `group_len`: the new-token counts sum to 3584.
All inputs are finite; a program needn't handle non-finite values.
Results may differ from a plain program's by a relative error of at most 0.0075.
The roundings to bfloat16 on the way count: a program that leaves them out, or rounds other values in their place, can miss the bound.
Values may be sent and summed in bfloat16 or wider, within the bound.
No kernel may reach another device: no remote copies, remote signals or barrier semaphores. Data moves between devices by JAX's collectives and lax.ppermute only.
A program may use at most 128 MiB of HBM per device.

v0:
```python
import jax
import jax.numpy as jnp
from jax import lax
from jax.sharding import PartitionSpec as P

HD = 128


def rotate(vector, position):
    half_dim = vector.shape[-1] // 2
    frequency = 1000000.0 ** (-(jnp.arange(half_dim, dtype=jnp.float32) * 2.0 / vector.shape[-1]))
    angles = position.astype(jnp.float32)[..., None] * frequency
    cosine = jnp.concatenate([jnp.cos(angles), jnp.cos(angles)], -1)[..., None, :]
    sine = jnp.concatenate([jnp.sin(angles), jnp.sin(angles)], -1)[..., None, :]
    turned = jnp.concatenate([-vector[..., half_dim:], vector[..., :half_dim]], -1)
    return vector * cosine + turned * sine


def body(
    tokens,
    norm_gain,
    w_query,
    w_key,
    w_value,
    w_out,
    cache_keys,
    cache_values,
    cache_len,
    group_len,
):
    seq_index = lax.axis_index("seq")
    seq_count = lax.axis_size("seq")
    requests, local_rows, width_part = tokens.shape
    heads_width = w_query.shape[1]
    local_heads = heads_width // HD
    cache_slots = cache_keys.shape[1]
    gain = norm_gain.astype(jnp.float32)
    offsets = jnp.arange(local_rows, dtype=jnp.int32)
    token_index = seq_index * local_rows + offsets
    slot_index = seq_index * cache_slots + jnp.arange(cache_slots, dtype=jnp.int32)
    query_index = jnp.arange(seq_count * local_rows, dtype=jnp.int32)
    score_scale = HD ** (-0.5)
    numer_width = local_rows * heads_width
    mixed_list = []
    key_list = []
    value_list = []
    for request in range(requests):
        gathered = lax.all_gather(tokens[request], "tensor", axis=1, tiled=True).astype(jnp.float32)
        inverse_rms = lax.rsqrt(jnp.mean(gathered * gathered, -1, keepdims=True) + 1e-05)
        normed = (gathered * inverse_rms * gain).astype(jnp.bfloat16)

        def project(weight):
            return jnp.dot(normed, weight, preferred_element_type=jnp.float32).reshape(
                local_rows, local_heads, HD
            )

        position = cache_len[request] + token_index
        queries = rotate(project(w_query)[None], position[None])[0].astype(jnp.bfloat16)
        key_new = rotate(project(w_key)[None], position[None])[0].astype(jnp.bfloat16)
        value_new = project(w_value).astype(jnp.bfloat16)
        live_rows = token_index < group_len[request]
        key_list.append(
            jnp.where(live_rows[:, None], key_new.reshape(local_rows, heads_width), 0.0).astype(
                jnp.bfloat16
            )
        )
        value_list.append(
            jnp.where(live_rows[:, None], value_new.reshape(local_rows, heads_width), 0.0).astype(
                jnp.bfloat16
            )
        )
        all_queries = lax.all_gather(queries, "seq", axis=0, tiled=True)
        cache_k = cache_keys[request].reshape(cache_slots, local_heads, HD)
        cache_v = cache_values[request].reshape(cache_slots, local_heads, HD)
        cache_ok = (slot_index < cache_len[request])[None, None, :]
        group_ok = ((token_index[None, :] <= query_index[:, None]) & live_rows[None, :])[None]
        cache_scores = jnp.where(
            cache_ok,
            jnp.einsum("qhd,khd->hqk", all_queries, cache_k, preferred_element_type=jnp.float32)
            * score_scale,
            -1e30,
        )
        group_scores = jnp.where(
            group_ok,
            jnp.einsum("qhd,khd->hqk", all_queries, key_new, preferred_element_type=jnp.float32)
            * score_scale,
            -1e30,
        )
        row_peak = jnp.maximum(jnp.max(cache_scores, -1), jnp.max(group_scores, -1))
        cache_weights = jnp.where(cache_ok, jnp.exp(cache_scores - row_peak[..., None]), 0.0)
        group_weights = jnp.where(group_ok, jnp.exp(group_scores - row_peak[..., None]), 0.0)
        row_mass = jnp.sum(cache_weights, -1) + jnp.sum(group_weights, -1)
        numerators = jnp.einsum(
            "hqk,khd->qhd",
            cache_weights.astype(jnp.bfloat16),
            cache_v,
            preferred_element_type=jnp.float32,
        ) + jnp.einsum(
            "hqk,khd->qhd",
            group_weights.astype(jnp.bfloat16),
            value_new,
            preferred_element_type=jnp.float32,
        )
        stats = jnp.stack([row_peak.T, row_mass.T], -1)
        payload = jnp.concatenate(
            [
                numerators.reshape(seq_count, numer_width),
                stats.reshape(seq_count, local_rows * local_heads * 2),
            ],
            -1,
        )
        received = lax.all_to_all(payload, "seq", 0, 0, tiled=True)
        block_numer = received[:, :numer_width].reshape(seq_count, local_rows, local_heads, HD)
        block_stats = received[:, numer_width:].reshape(seq_count, local_rows, local_heads, 2)
        block_peak = block_stats[..., 0]
        factor = jnp.exp(block_peak - jnp.max(block_peak, 0))
        numer_sum = jnp.sum(block_numer * factor[..., None], 0)
        mass_sum = jnp.sum(block_stats[..., 1] * factor, 0)
        attended = numer_sum / mass_sum[..., None]
        attended = (
            jnp.where(live_rows[:, None, None], attended, 0.0)
            .astype(jnp.bfloat16)
            .reshape(local_rows, heads_width)
        )
        partial_out = jnp.dot(attended, w_out, preferred_element_type=jnp.float32)
        mixed_list.append(
            lax.psum_scatter(partial_out, "tensor", scatter_dimension=1, tiled=True).astype(
                jnp.bfloat16
            )
        )
    return (jnp.stack(mixed_list), jnp.stack(key_list), jnp.stack(value_list))


def solution(mesh):
    placed = (
        P(None, "seq", "tensor"),
        P(),
        P(None, "tensor"),
        P(None, "tensor"),
        P(None, "tensor"),
        P("tensor", None),
        P(None, "seq", "tensor"),
        P(None, "seq", "tensor"),
        P(),
        P(),
    )
    return jax.shard_map(
        body,
        mesh=mesh,
        in_specs=placed,
        out_specs=(P(None, "seq", "tensor"), P(None, "seq", "tensor"), P(None, "seq", "tensor")),
        check_vma=False,
    )
```

profile of v0, /device:TPU:4, one launch (start us, length us, event | category | flops | bytes accessed | tf_op | source)
XLA Modules:
  0.0 626.7 jit_solution(12570984559530962175)
XLA Ops:
  7.2 1.5 fusion.236
  9.2 1.3 add_convert_fusion
  10.6 1.3 add_convert_fusion.2
  13.7 1.4 fusion.222
  15.1 29.1 %all-gather = bf16[1,32,4096]{2,1,0:T(8,128)(2,1)S(1)} all-gather(bf16[1,32,512]{2,1,0:T(8,128)(2,1)S(1)} %get-tuple-element.11), channel_id=2, replica_groups=mesh['seq'=32,'tensor'=8] {'tensor'}, dimensions={2}, use_global_device_ids=true | all-gather | bytes 294912 | tf_op jit(solution)/shard_map/all_gather | solution.py:48
  44.3 2.1 fusion.216
  46.6 2.1 fusion.218
  49.6 43.6 %all_gather.25 = bf16[1024,2,128]{2,0,1:T(8,128)(2,1)S(1)} all-gather(bf16[32,2,128]{2,0,1:T(8,128)(2,1)S(1)} %get-tuple-element.44), channel_id=1, replica_groups=mesh['seq'=32,'tensor'=8] {'seq'}, dimensions={0}, use_global_device_ids=true | all-gather | bytes 540672 | tf_op jit(solution)/shard_map/all_gather | solution.py:72
  93.2 1.5 fusion.235
  96.9 1.2 broadcast_compare_fusion.2
  102.3 1.8 fusion.220
  111.9 1.8 copy.232
  113.7 2.1 reshape.925
  115.8 1.3 copy.233
  117.1 2.5 reshape.926
  119.7 2.1 copy.234
  121.8 7.4 %all-to-all-start = ((f32[32,1,8320]{2,1,0:T(1,128)}), f32[32,1,8320]{2,1,0:T(1,128)}, u32[]{:S(2)}, u32[]{:S(2)}) async-start(f32[32,1,8320]{2,1,0:T(1,128)} %copy.234), calls=%async_computation | async-start | bytes 2129920 | tf_op jit(solution)/shard_map/all_to_all | solution.py:112
  129.2 30.6 %all-gather.1 = bf16[1,32,4096]{2,1,0:T(8,128)(2,1)S(1)} all-gather(bf16[1,32,512]{2,1,0:T(8,128)(2,1)S(1)} %copy-done.49), channel_id=3, replica_groups=mesh['seq'=32,'tensor'=8] {'tensor'}, dimensions={2}, use_global_device_ids=true | all-gather | bytes 294912 | tf_op jit(solution)/shard_map/all_gather | solution.py:48
  159.9 2.2 fusion.211
  162.7 1.3 fusion.170
  165.1 29.0 %all-gather.2 = bf16[1,32,4096]{2,1,0:T(8,128)(2,1)S(1)} all-gather(bf16[1,32,512]{2,1,0:T(8,128)(2,1)S(1)} %copy-done.48), channel_id=4, replica_groups=mesh['seq'=32,'tensor'=8] {'tensor'}, dimensions={2}, use_global_device_ids=true | all-gather | bytes 294912 | tf_op jit(solution)/shard_map/all_gather | solution.py:48
  198.8 28.7 %all-gather.3 = bf16[1,32,4096]{2,1,0:T(8,128)(2,1)S(1)} all-gather(bf16[1,32,512]{2,1,0:T(8,128)(2,1)S(1)} %copy-done.47), channel_id=5, replica_groups=mesh['seq'=32,'tensor'=8] {'tensor'}, dimensions={2}, use_global_device_ids=true | all-gather | bytes 294912 | tf_op jit(solution)/shard_map/all_gather | solution.py:48
  230.6 39.5 %all_gather.27 = bf16[1024,2,128]{2,0,1:T(8,128)(2,1)S(1)} all-gather(bf16[32,2,128]{2,0,1:T(8,128)(2,1)S(1)} %get-tuple-element.46), channel_id=1, replica_groups=mesh['seq'=32,'tensor'=8] {'seq'}, dimensions={0}, use_global_device_ids=true | all-gather | bytes 540672 | tf_op jit(solution)/shard_map/all_gather | solution.py:72
  276.4 1.8 copy.251
  278.2 2.1 reshape.928
  281.0 1.3 pad_maximum_fusion.4
  282.3 2.0 copy.252
  284.3 3.1 reshape.929
  288.2 2.1 copy.253
  291.5 38.3 %all_gather.29 = bf16[1024,2,128]{2,0,1:T(8,128)(2,1)S(1)} all-gather(bf16[32,2,128]{2,0,1:T(8,128)(2,1)S(1)} %get-tuple-element.48), channel_id=1, replica_groups=mesh['seq'=32,'tensor'=8] {'seq'}, dimensions={0}, use_global_device_ids=true | all-gather | bytes 540672 | tf_op jit(solution)/shard_map/all_gather | solution.py:72
  333.0 1.8 fusion.12
  337.6 1.8 reshape.931
  340.1 1.3 pad_maximum_fusion.5
  341.4 1.2 copy.271
  342.6 1.9 reshape.932
  347.2 39.4 %all_gather.31 = bf16[1024,2,128]{2,0,1:T(8,128)(2,1)S(1)} all-gather(bf16[32,2,128]{2,0,1:T(8,128)(2,1)S(1)} %get-tuple-element.50), channel_id=1, replica_groups=mesh['seq'=32,'tensor'=8] {'seq'}, dimensions={0}, use_global_device_ids=true | all-gather | bytes 540672 | tf_op jit(solution)/shard_map/all_gather | solution.py:72
  386.7 2.3 maximum_bitcast_fusion.2
  389.0 8.5 %all-to-all-start.1 = ((f32[32,1,8320]{2,1,0:T(1,128)}), f32[32,1,8320]{2,1,0:T(1,128)}, u32[]{:S(2)}, u32[]{:S(2)}) async-start(f32[32,1,8320]{2,1,0:T(1,128)} %copy.253), calls=%async_computation.2 | async-start | bytes 2129920 | tf_op jit(solution)/shard_map/all_to_all | solution.py:112
  397.8 3.4 copy.272
  406.5 1.8 reshape.934
  408.4 2.2 fusion.14
  411.2 1.3 reshape.935
  412.5 12.4 %all-to-all-done.1 = f32[32,1,8320]{2,1,0:T(1,128)} async-done(((f32[32,1,8320]{2,1,0:T(1,128)}), f32[32,1,8320]{2,1,0:T(1,128)}, u32[]{:S(2)}, u32[]{:S(2)}) %all-to-all-start.1) | async-done | bytes 1064992 | tf_op jit(solution)/shard_map/all_to_all | solution.py:112
  424.9 6.7 %all-to-all-start.2 = ((f32[32,1,8320]{2,1,0:T(1,128)}), f32[32,1,8320]{2,1,0:T(1,128)S(1)}, u32[]{:S(2)}, u32[]{:S(2)}) async-start(f32[32,1,8320]{2,1,0:T(1,128)} %copy.272), calls=%async_computation.4 | async-start | bytes 2129920 | tf_op jit(solution)/shard_map/all_to_all | solution.py:112
  431.6 1.3 maximum_bitcast_fusion.3
  432.9 2.1 copy.291
  435.0 5.1 copy.235
  441.3 3.3 fusion.3
  445.0 1.4 fusion.132
  446.5 5.1 copy.254
  452.4 6.9 %all-to-all-done.2 = f32[32,1,8320]{2,1,0:T(1,128)S(1)} async-done(((f32[32,1,8320]{2,1,0:T(1,128)}), f32[32,1,8320]{2,1,0:T(1,128)S(1)}, u32[]{:S(2)}, u32[]{:S(2)}) %all-to-all-start.2) | async-done | bytes 1064992 | tf_op jit(solution)/shard_map/all_to_all | solution.py:112
  459.3 7.2 %all-to-all-start.3 = ((f32[32,1,8320]{2,1,0:T(1,128)}), f32[32,1,8320]{2,1,0:T(1,128)}, u32[]{:S(2)}, u32[]{:S(2)}) async-start(f32[32,1,8320]{2,1,0:T(1,128)} %copy.291), calls=%async_computation.6 | async-start | bytes 2129920 | tf_op jit(solution)/shard_map/all_to_all | solution.py:112
  467.2 3.3 fusion.2
  470.9 1.3 fusion.134
  472.4 3.7 copy.273
  477.3 3.3 fusion.1
  481.0 1.3 fusion.136
  482.6 11.5 %all-to-all-done.3 = f32[32,1,8320]{2,1,0:T(1,128)} async-done(((f32[32,1,8320]{2,1,0:T(1,128)}), f32[32,1,8320]{2,1,0:T(1,128)}, u32[]{:S(2)}, u32[]{:S(2)}) %all-to-all-start.3) | async-done | bytes 1064992 | tf_op jit(solution)/shard_map/all_to_all | solution.py:112
  494.1 5.1 copy.292
  500.3 3.3 fusion
  504.0 1.3 fusion.138
  507.6 25.9 %reduce-scatter.7.cloned.1.call-done = f32[32,512]{1,0:T(8,128)} async-done(((f32[32,4096]{1,0:T(8,128)}), f32[32,512]{1,0:T(8,128)}) %reduce-scatter.7.cloned.1.call-update) | async-done | bytes 65552 | tf_op jit(solution)/shard_map/reduce_scatter | solution.py:127
  534.3 41.6 %reduce-scatter.9.cloned.1.call-done = f32[32,512]{1,0:T(8,128)} async-done(((f32[32,4096]{1,0:T(8,128)}), f32[32,512]{1,0:T(8,128)}) %reduce-scatter.9.cloned.1.call-update) | async-done | bytes 65552 | tf_op jit(solution)/shard_map/reduce_scatter | solution.py:127
  576.8 41.4 %reduce-scatter.11.cloned.1.call-done = f32[32,512]{1,0:T(8,128)} async-done(((f32[32,4096]{1,0:T(8,128)}), f32[32,512]{1,0:T(8,128)}) %reduce-scatter.11.cloned.1.call-update) | async-done | bytes 65552 | tf_op jit(solution)/shard_map/reduce_scatter | solution.py:127
  (293 shorter events, 63.5 us)
Async XLA Ops:
  7.2 437.8 %copy-start = (bf16[256,4096]{1,0:T(8,128)(2,1)S(1)}, bf16[256,4096]{1,0:T(8,128)(2,1)}, u32[]{:S(2)}) copy-start(bf16[256,4096]{1,0:T(8,128)(2,1)} %param.15) | copy-start | bytes 6291460
  12.9 36.0 %copy-start.21 = (f32[32,128]{1,0:T(8,128)}, f32[32,128]{1,0:T(8,128)S(1)}, u32[]{:S(2)}) copy-start(f32[32,128]{1,0:T(8,128)S(1)} %maximum_bitcast_fusion.4) | copy-start | bytes 49156
  12.9 36.0 %copy-start.37 = (f32[32,128]{1,0:T(8,128)}, f32[32,128]{1,0:T(8,128)S(1)}, u32[]{:S(2)}) copy-start(f32[32,128]{1,0:T(8,128)S(1)} %maximum_bitcast_fusion.5) | copy-start | bytes 49156
  44.3 2.2 copy-start.60
  46.4 54.1 %copy-start.11 = (bf16[4,256,256]{2,1,0:T(8,128)(2,1)S(1)}, bf16[4,256,256]{2,1,0:T(8,128)(2,1)}, u32[]{:S(2)}) copy-start(bf16[4,256,256]{2,1,0:T(8,128)(2,1)} %param.16) | copy-start | bytes 1572868
  48.9 55.3 %copy-start.19 = (f32[32,2,64]{2,0,1:T(8,128)}, f32[32,2,64]{2,0,1:T(8,128)S(1)}, u32[]{:S(2)}) copy-start(f32[32,2,64]{2,0,1:T(8,128)S(1)} %get-tuple-element.118) | copy-start | bytes 49156
  106.9 2.5 copy-start.40
  106.9 2.5 copy-start.64
  111.4 2.3 copy-start.35
  119.7 9.5 %copy-start.49 = (bf16[1,32,512]{2,1,0:T(8,128)(2,1)S(1)}, bf16[1,32,512]{2,1,0:T(8,128)(2,1)}, u32[]{:S(2)}) copy-start(bf16[1,32,512]{2,1,0:T(8,128)(2,1)} %get-tuple-element.12) | copy-start | bytes 98308
  121.8 267.2 %all-to-all-start = ((f32[32,1,8320]{2,1,0:T(1,128)}), f32[32,1,8320]{2,1,0:T(1,128)}, u32[]{:S(2)}, u32[]{:S(2)}) async-start(f32[32,1,8320]{2,1,0:T(1,128)} %copy.234), calls=%async_computation | async-start | bytes 2129920 | tf_op jit(solution)/shard_map/all_to_all | solution.py:112
  129.1 33.0 %copy-start.2 = (bf16[4096,256]{1,0:T(8,128)(2,1)S(1)}, bf16[4096,256]{1,0:T(8,128)(2,1)}, u32[]{:S(2)}) copy-start(bf16[4096,256]{1,0:T(8,128)(2,1)} %param.12) | copy-start | bytes 6291460
  159.9 4.1 copy-start.4
  162.2 108.8 %copy-start.9 = (f32[32,256]{1,0:T(8,128)}, f32[32,256]{1,0:T(8,128)S(1)}, u32[]{:S(2)}) copy-start(f32[32,256]{1,0:T(8,128)S(1)} %fusion.211) | copy-start | bytes 98308
  162.2 2.9 copy-start.48
  162.2 32.1 %copy-start.1 = (bf16[4096,256]{1,0:T(8,128)(2,1)S(1)}, bf16[4096,256]{1,0:T(8,128)(2,1)}, u32[]{:S(2)}) copy-start(bf16[4096,256]{1,0:T(8,128)(2,1)} %param.13) | copy-start | bytes 6291460
  195.5 3.4 copy-start.47
  227.7 1.8 copy-start.52
  228.3 41.8 %copy-start.15 = (bf16[1,256,256]{2,1,0:T(8,128)(2,1)S(1)}, bf16[1,256,256]{2,1,0:T(8,128)(2,1)}, u32[]{:S(2)}) copy-start(bf16[1,256,256]{2,1,0:T(8,128)(2,1)} %get-tuple-element.9) | copy-start | bytes 393220
  228.3 41.9 %copy-start.16 = (bf16[1,256,256]{2,1,0:T(8,128)(2,1)S(1)}, bf16[1,256,256]{2,1,0:T(8,128)(2,1)}, u32[]{:S(2)}) copy-start(bf16[1,256,256]{2,1,0:T(8,128)(2,1)} %get-tuple-element.5) | copy-start | bytes 393220
  229.5 40.6 %copy-start.23 = (f32[32,128]{1,0:T(8,128)}, f32[32,128]{1,0:T(8,128)S(1)}, u32[]{:S(2)}) copy-start(f32[32,128]{1,0:T(8,128)S(1)} %maximum_bitcast_fusion.6) | copy-start | bytes 49156
  229.6 40.5 %copy-start.38 = (f32[32,128]{1,0:T(8,128)}, f32[32,128]{1,0:T(8,128)S(1)}, u32[]{:S(2)}) copy-start(f32[32,128]{1,0:T(8,128)S(1)} %maximum_bitcast_fusion.7) | copy-start | bytes 49156
  229.8 40.2 %copy-start.20 = (f32[32,2,64]{2,0,1:T(8,128)}, f32[32,2,64]{2,0,1:T(8,128)S(1)}, u32[]{:S(2)}) copy-start(f32[32,2,64]{2,0,1:T(8,128)S(1)} %get-tuple-element.114) | copy-start | bytes 49156
  270.1 3.2 copy-start.63
  272.1 2.4 copy-start.41
  273.3 2.8 copy-start.29
  287.4 2.9 copy-start.51
  287.4 3.0 copy-start.50
  288.2 2.3 copy-start.7
  288.2 2.4 copy-start.18
  288.2 41.6 %copy-start.13 = (bf16[1,256,256]{2,1,0:T(8,128)(2,1)S(1)}, bf16[1,256,256]{2,1,0:T(8,128)(2,1)}, u32[]{:S(2)}) copy-start(bf16[1,256,256]{2,1,0:T(8,128)(2,1)} %get-tuple-element.8) | copy-start | bytes 393220
  288.2 41.7 %copy-start.14 = (bf16[1,256,256]{2,1,0:T(8,128)(2,1)S(1)}, bf16[1,256,256]{2,1,0:T(8,128)(2,1)}, u32[]{:S(2)}) copy-start(bf16[1,256,256]{2,1,0:T(8,128)(2,1)} %get-tuple-element.4) | copy-start | bytes 393220
  290.4 39.4 %copy-start.25 = (f32[32,128]{1,0:T(8,128)}, f32[32,128]{1,0:T(8,128)S(1)}, u32[]{:S(2)}) copy-start(f32[32,128]{1,0:T(8,128)S(1)} %maximum_bitcast_fusion.8) | copy-start | bytes 49156
  290.5 39.3 %copy-start.39 = (f32[32,128]{1,0:T(8,128)}, f32[32,128]{1,0:T(8,128)S(1)}, u32[]{:S(2)}) copy-start(f32[32,128]{1,0:T(8,128)S(1)} %maximum_bitcast_fusion.9) | copy-start | bytes 49156
  331.8 3.1 copy-start.42
  331.8 3.0 copy-start.62
  333.0 3.4 copy-start.30
  337.5 8.0 %copy-start.17 = (f32[32,256]{1,0:T(8,128)S(1)}, f32[32,256]{1,0:T(8,128)}, u32[]{:S(2)}) copy-start(f32[32,256]{1,0:T(8,128)} %fusion.203) | copy-start | bytes 98308
  345.4 52.1 %copy-start.27 = (f32[32,128]{1,0:T(8,128)}, f32[32,128]{1,0:T(8,128)S(1)}, u32[]{:S(2)}) copy-start(f32[32,128]{1,0:T(8,128)S(1)} %maximum_bitcast_fusion.10) | copy-start | bytes 49156
  389.0 12.2 %copy-start.12 = (bf16[1,256,256]{2,1,0:T(8,128)(2,1)S(1)}, bf16[1,256,256]{2,1,0:T(8,128)(2,1)}, u32[]{:S(2)}) copy-start(bf16[1,256,256]{2,1,0:T(8,128)(2,1)} %get-tuple-element.10) | copy-start | bytes 393220
  389.0 35.9 %all-to-all-start.1 = ((f32[32,1,8320]{2,1,0:T(1,128)}), f32[32,1,8320]{2,1,0:T(1,128)}, u32[]{:S(2)}, u32[]{:S(2)}) async-start(f32[32,1,8320]{2,1,0:T(1,128)} %copy.253), calls=%async_computation.2 | async-start | bytes 2129920 | tf_op jit(solution)/shard_map/all_to_all | solution.py:112
  401.2 2.5 copy-start.59
  405.7 2.7 copy-start.66
  424.9 34.4 %all-to-all-start.2 = ((f32[32,1,8320]{2,1,0:T(1,128)}), f32[32,1,8320]{2,1,0:T(1,128)S(1)}, u32[]{:S(2)}, u32[]{:S(2)}) async-start(f32[32,1,8320]{2,1,0:T(1,128)} %copy.272), calls=%async_computation.4 | async-start | bytes 2129920 | tf_op jit(solution)/shard_map/all_to_all | solution.py:112
  431.6 75.1 %reduce-scatter.5.cloned.1.call-start = ((), (), s32[]{:S(2)}) async-start(), calls=%async_computation.8 | async-start | bytes 589824 | tf_op jit(solution)/shard_map/reduce_scatter | solution.py:127
  441.3 3.7 copy-start.57
  444.6 1.8 copy-start.22
  444.6 1.8 copy-start.36
  444.6 1.8 copy-start.43
  459.3 34.8 %all-to-all-start.3 = ((f32[32,1,8320]{2,1,0:T(1,128)}), f32[32,1,8320]{2,1,0:T(1,128)}, u32[]{:S(2)}, u32[]{:S(2)}) async-start(f32[32,1,8320]{2,1,0:T(1,128)} %copy.291), calls=%async_computation.6 | async-start | bytes 2129920 | tf_op jit(solution)/shard_map/all_to_all | solution.py:112
  466.5 67.0 %reduce-scatter.7.cloned.1.call-start = ((), (), s32[]{:S(2)}) async-start(), calls=%async_computation.9 | async-start | bytes 589824 | tf_op jit(solution)/shard_map/reduce_scatter | solution.py:127
  467.2 3.7 copy-start.56
  470.5 1.8 copy-start.24
  470.5 1.8 copy-start.10
  470.5 1.8 copy-start.34
  470.6 1.8 copy-start.44
  472.2 103.7 %reduce-scatter.9.cloned.1.call-start = ((), (), s32[]{:S(2)}) async-start(), calls=%async_computation.10 | async-start | bytes 589824 | tf_op jit(solution)/shard_map/reduce_scatter | solution.py:127
  477.3 3.7 copy-start.55
  480.7 1.7 copy-start.26
  480.7 1.8 copy-start.8
  480.7 1.8 copy-start.32
  480.7 1.8 copy-start.45
  482.4 135.8 %reduce-scatter.11.cloned.1.call-start = ((), (), s32[]{:S(2)}) async-start(), calls=%async_computation.11 | async-start | bytes 589824 | tf_op jit(solution)/shard_map/reduce_scatter | solution.py:127
  500.3 3.7 copy-start.54
  (11 other events, 17.5 us)
Sparse Core Ops, SparseCore 0:
  446.5 43.2 reduce-scatter.4
  492.3 41.1 reduce-scatter.6
  536.0 39.8 reduce-scatter.8
  578.3 39.8 reduce-scatter.10
where the time goes:
time: 637 us; the launch traced here: 627 us
  blocking collectives  278 us (44%)
  waiting for transfers between devices  140 us (22%)
  local copies, waits for them, and re-layouts  72.8 us (11%)
  other arithmetic  58.1 us (9%)
  matrix products  32 us (5%)
  starting transfers between devices  30.2 us (5%)
  between operations  15.7 us (2%)
    all_gather x4, blocking collectives, body(): all_queries = lax.all_gather(queries, 'seq', axis=0, tiled=True)  161 us
    all_gather x4, blocking collectives, body(): lax.all_gather(tokens[request], 'tensor', axis=1, tiled=True)  117 us
    reduce_scatter x4, waiting for transfers between devices, body(): lax.psum_scatter(partial_out, 'tensor', scatter_dimension=1, tiled=True)  109 us
    all_to_all x4, waiting for transfers between devices, body(): received = lax.all_to_all(payload, 'seq', 0, 0, tiled=True)  30.8 us
    all_to_all x4, starting transfers between devices, body(): received = lax.all_to_all(payload, 'seq', 0, 0, tiled=True)  29.7 us
    all_to_all x8, local copies, waits for them, and re-layouts, body(): received = lax.all_to_all(payload, 'seq', 0, 0, tiled=True)  28.6 us
    dot_general x12, matrix products, project(): jnp.dot(normed, weight, preferred_element_type=jnp.float32)  14.1 us
    reduce_sum x4, other arithmetic, body(): numer_sum = jnp.sum(block_numer * factor[..., None], 0)  13.4 us
  transfers between devices with their start and end apart: 8, of which 6 were waited for; matrix products, arithmetic and copies ran while one was open for 19% of the time, Pallas kernels for 0%

commit v1 on v0

--- a/solution.py
+++ b/solution.py
@@ -69,7 +69,20 @@
                 jnp.bfloat16
             )
         )
-        all_queries = lax.all_gather(queries, "seq", axis=0, tiled=True)
+
+        def pass_modes_over_axis(axis_no, device_axis, original):
+            main = jnp.concatenate(
+                lax.all_to_all(
+                    jnp.stack(tuple((original for _ in range(lax.axis_size(device_axis)))), axis=0),
+                    axis_name=device_axis,
+                    split_axis=0,
+                    concat_axis=0,
+                ),
+                axis=axis_no,
+            )
+            return main
+
+        all_queries = pass_modes_over_axis(0, "seq", original=queries)
         cache_k = cache_keys[request].reshape(cache_slots, local_heads, HD)
         cache_v = cache_values[request].reshape(cache_slots, local_heads, HD)
         cache_ok = (slot_index < cache_len[request])[None, None, :]

time: 637 us -> 578 us (0.907)
  blocking collectives: 278 us -> 116 us
  starting transfers between devices: 30.2 us -> 68.9 us
  waiting for transfers between devices: 140 us -> 174 us
  local copies, waits for them, and re-layouts: 72.8 us -> 92 us
  other arithmetic: 58.1 us -> 66.5 us
    all_gather x4 -> x0, blocking collectives: 161 us -> none  [body(): all_queries = lax.all_gather(queries, 'seq', axis=0, tiled=True)]
    all_to_all x0 -> x4, starting transfers between devices: none -> 36.9 us  [pass_modes_over_axis(): lax.all_to_all(jnp.stack(tuple((original for _ in range(lax.axis_size(dev...]
    all_to_all x0 -> x4, waiting for transfers between devices: none -> 21.9 us  [pass_modes_over_axis(): lax.all_to_all(jnp.stack(tuple((original for _ in range(lax.axis_size(dev...]
    all_to_all x4, waiting for transfers between devices: 30.8 us -> 38.2 us  [body(): received = lax.all_to_all(payload, 'seq', 0, 0, tiled=True)]
  transfers between devices with their start and end apart: 8 -> 12, of which waited for: 6 -> 9; matrix products, arithmetic and copies ran while one was open for 19% -> 30% of each run, Pallas kernels for 0% -> 0%
where the time goes in v1:
time: 578 us; the launch traced here: 568 us
  waiting for transfers between devices  174 us (30%)
  blocking collectives  116 us (20%)
  local copies, waits for them, and re-layouts  92 us (16%)
  starting transfers between devices  68.9 us (12%)
  other arithmetic  66.5 us (12%)
  matrix products  33.8 us (6%)
  between operations  16 us (3%)
    all_gather x4, blocking collectives, body(): lax.all_gather(tokens[request], 'tensor', axis=1, tiled=True)  116 us
    reduce_scatter x4, waiting for transfers between devices, body(): lax.psum_scatter(partial_out, 'tensor', scatter_dimension=1, tiled=True)  114 us
    all_to_all x4, waiting for transfers between devices, body(): received = lax.all_to_all(payload, 'seq', 0, 0, tiled=True)  38.2 us
    all_to_all x4, starting transfers between devices, pass_modes_over_axis(): lax.all_to_all(jnp.stack(tuple((original for _ in range(lax.axis_size(dev...  36.9 us
    all_to_all x4, starting transfers between devices, body(): received = lax.all_to_all(payload, 'seq', 0, 0, tiled=True)  31.6 us
    all_to_all x8, local copies, waits for them, and re-layouts, body(): received = lax.all_to_all(payload, 'seq', 0, 0, tiled=True)  26.1 us
    all_to_all x4, waiting for transfers between devices, pass_modes_over_axis(): lax.all_to_all(jnp.stack(tuple((original for _ in range(lax.axis_size(dev...  21.9 us
    dot_general x12, matrix products, project(): jnp.dot(normed, weight, preferred_element_type=jnp.float32)  18.4 us
  transfers between devices with their start and end apart: 12, of which 9 were waited for; matrix products, arithmetic and copies ran while one was open for 30% of the time, Pallas kernels for 0%

profile of v1, /device:TPU:4, one launch (start us, length us, event | category | flops | bytes accessed | tf_op | source)
XLA Modules:
  0.0 567.7 jit_solution(16131164307123163412)
XLA Ops:
  7.2 1.5 fusion.236
  13.8 29.1 %all-gather = bf16[1,32,4096]{2,1,0:T(8,128)(2,1)S(1)} all-gather(bf16[1,32,512]{2,1,0:T(8,128)(2,1)S(1)} %get-tuple-element.11), channel_id=2, replica_groups=mesh['seq'=32,'tensor'=8] {'tensor'}, dimensions={2}, use_global_device_ids=true | all-gather | bytes 294912 | tf_op jit(solution)/shard_map/all_gather | solution.py:48
  43.1 2.1 fusion.216
  45.3 2.1 fusion.218
  49.2 11.6 %all-to-all-start = ((bf16[32,32,2,128]{3,1,2,0:T(8,128)(2,1)}), bf16[32,32,2,128]{3,1,2,0:T(8,128)(2,1)}, u32[]{:S(2)}, u32[]{:S(2)}) async-start(bf16[32,32,2,128]{3,1,2,0:T(8,128)(2,1)} %stack.62), calls=%async_computation | async-start | bytes 1048576 | tf_op jit(solution)/shard_map/all_to_all | solution.py:75
  61.5 29.2 %all-gather.1 = bf16[1,32,4096]{2,1,0:T(8,128)(2,1)S(1)} all-gather(bf16[1,32,512]{2,1,0:T(8,128)(2,1)S(1)} %get-tuple-element.12), channel_id=3, replica_groups=mesh['seq'=32,'tensor'=8] {'tensor'}, dimensions={2}, use_global_device_ids=true | all-gather | bytes 294912 | tf_op jit(solution)/shard_map/all_gather | solution.py:48
  90.9 2.1 fusion.211
  96.6 29.0 %all-gather.2 = bf16[1,32,4096]{2,1,0:T(8,128)(2,1)S(1)} all-gather(bf16[1,32,512]{2,1,0:T(8,128)(2,1)S(1)} %get-tuple-element.14), channel_id=4, replica_groups=mesh['seq'=32,'tensor'=8] {'tensor'}, dimensions={2}, use_global_device_ids=true | all-gather | bytes 294912 | tf_op jit(solution)/shard_map/all_gather | solution.py:48
  125.8 2.2 fusion.206
  129.2 28.9 %all-gather.3 = bf16[1,32,4096]{2,1,0:T(8,128)(2,1)S(1)} all-gather(bf16[1,32,512]{2,1,0:T(8,128)(2,1)S(1)} %get-tuple-element.13), channel_id=5, replica_groups=mesh['seq'=32,'tensor'=8] {'tensor'}, dimensions={2}, use_global_device_ids=true | all-gather | bytes 294912 | tf_op jit(solution)/shard_map/all_gather | solution.py:48
  172.2 1.5 maximum_bitcast_fusion.9
  176.8 1.5 maximum_bitcast_fusion.11
  183.9 1.4 select_bitcast_fusion.3
  186.8 1.4 fusion.174
  188.2 1.4 fusion.173
  189.6 1.4 fusion.172
  193.2 1.7 copy.346
  194.9 1.7 copy.349
  196.5 1.7 copy.352
  199.0 1.7 copy.358
  200.7 1.7 copy.364
  203.8 2.7 convolution_convert_fusion.2
  209.7 10.2 %all-to-all-start.2 = ((bf16[32,32,2,128]{3,1,2,0:T(8,128)(2,1)}), bf16[32,32,2,128]{3,1,2,0:T(8,128)(2,1)}, u32[]{:S(2)}, u32[]{:S(2)}) async-start(bf16[32,32,2,128]{3,1,2,0:T(8,128)(2,1)} %stack.67), calls=%async_computation.3 | async-start | bytes 1048576 | tf_op jit(solution)/shard_map/all_to_all | solution.py:75
  223.3 1.8 copy.247
  225.0 2.1 reshape.982
  228.0 2.2 fusion.8
  231.5 2.5 reshape.983
  234.0 2.9 all-to-all-done.2
  237.9 7.3 %all-to-all-start.4 = ((bf16[32,32,2,128]{3,1,2,0:T(8,128)(2,1)}), bf16[32,32,2,128]{3,1,2,0:T(8,128)(2,1)}, u32[]{:S(2)}, u32[]{:S(2)}) async-start(bf16[32,32,2,128]{3,1,2,0:T(8,128)(2,1)} %stack.72), calls=%async_computation.6 | async-start | bytes 1048576 | tf_op jit(solution)/shard_map/all_to_all | solution.py:75
  245.3 2.1 copy.249
  251.7 10.6 %all-to-all-done.4 = bf16[32,32,2,128]{3,1,2,0:T(8,128)(2,1)} async-done(((bf16[32,32,2,128]{3,1,2,0:T(8,128)(2,1)}), bf16[32,32,2,128]{3,1,2,0:T(8,128)(2,1)}, u32[]{:S(2)}, u32[]{:S(2)}) %all-to-all-start.4) | async-done | bytes 524320 | tf_op jit(solution)/shard_map/all_to_all | solution.py:75
  262.3 1.6 stack.77
  263.9 7.7 %all-to-all-start.6 = ((bf16[32,32,2,128]{3,1,2,0:T(8,128)(2,1)}), bf16[32,32,2,128]{3,1,2,0:T(8,128)(2,1)}, u32[]{:S(2)}, u32[]{:S(2)}) async-start(bf16[32,32,2,128]{3,1,2,0:T(8,128)(2,1)} %stack.77), calls=%async_computation.9 | async-start | bytes 1048576 | tf_op jit(solution)/shard_map/all_to_all | solution.py:75
  273.7 1.8 reshape.986
  276.3 2.2 fusion.10
  280.4 8.3 %all-to-all-done.6 = bf16[32,32,2,128]{3,1,2,0:T(8,128)(2,1)} async-done(((bf16[32,32,2,128]{3,1,2,0:T(8,128)(2,1)}), bf16[32,32,2,128]{3,1,2,0:T(8,128)(2,1)}, u32[]{:S(2)}, u32[]{:S(2)}) %all-to-all-start.6) | async-done | bytes 524320 | tf_op jit(solution)/shard_map/all_to_all | solution.py:75
  288.7 6.8 %all-to-all-start.1 = ((f32[32,1,8320]{2,1,0:T(1,128)}), f32[32,1,8320]{2,1,0:T(1,128)S(1)}, u32[]{:S(2)}, u32[]{:S(2)}) async-start(f32[32,1,8320]{2,1,0:T(1,128)} %copy.249), calls=%async_computation.1 | async-start | bytes 2129920 | tf_op jit(solution)/shard_map/all_to_all | solution.py:125
  296.8 2.1 copy.269
  302.3 1.8 copy.287
  304.1 3.1 reshape.990
  308.0 2.2 fusion.12
  311.6 2.5 reshape.991
  314.1 8.9 %all-to-all-done.1 = f32[32,1,8320]{2,1,0:T(1,128)S(1)} async-done(((f32[32,1,8320]{2,1,0:T(1,128)}), f32[32,1,8320]{2,1,0:T(1,128)S(1)}, u32[]{:S(2)}, u32[]{:S(2)}) %all-to-all-start.1) | async-done | bytes 1064992 | tf_op jit(solution)/shard_map/all_to_all | solution.py:125
  323.0 7.7 %all-to-all-start.3 = ((f32[32,1,8320]{2,1,0:T(1,128)}), f32[32,1,8320]{2,1,0:T(1,128)}, u32[]{:S(2)}, u32[]{:S(2)}) async-start(f32[32,1,8320]{2,1,0:T(1,128)} %copy.269), calls=%async_computation.4 | async-start | bytes 2129920 | tf_op jit(solution)/shard_map/all_to_all | solution.py:125
  332.1 2.1 copy.289
  339.2 18.9 %all-to-all-done.3 = f32[32,1,8320]{2,1,0:T(1,128)} async-done(((f32[32,1,8320]{2,1,0:T(1,128)}), f32[32,1,8320]{2,1,0:T(1,128)}, u32[]{:S(2)}, u32[]{:S(2)}) %all-to-all-start.3) | async-done | bytes 1064992 | tf_op jit(solution)/shard_map/all_to_all | solution.py:125
  358.1 7.4 %all-to-all-start.5 = ((f32[32,1,8320]{2,1,0:T(1,128)}), f32[32,1,8320]{2,1,0:T(1,128)}, u32[]{:S(2)}, u32[]{:S(2)}) async-start(f32[32,1,8320]{2,1,0:T(1,128)} %copy.289), calls=%async_computation.7 | async-start | bytes 2129920 | tf_op jit(solution)/shard_map/all_to_all | solution.py:125
  365.6 3.0 copy.307
  368.6 3.1 reshape.994
  373.0 2.5 reshape.995
  375.5 3.8 copy.250
  380.4 3.3 fusion.3
  385.5 2.1 copy.309
  387.7 5.1 copy.270
  393.6 9.8 %all-to-all-start.7 = ((f32[32,1,8320]{2,1,0:T(1,128)}), f32[32,1,8320]{2,1,0:T(1,128)S(1)}, u32[]{:S(2)}, u32[]{:S(2)}) async-start(f32[32,1,8320]{2,1,0:T(1,128)} %copy.309), calls=%async_computation.10 | async-start | bytes 2129920 | tf_op jit(solution)/shard_map/all_to_all | solution.py:125
  404.1 3.3 fusion.2
  409.3 5.1 copy.290
  415.6 3.3 fusion.1
  420.8 10.3 %all-to-all-done.7 = f32[32,1,8320]{2,1,0:T(1,128)S(1)} async-done(((f32[32,1,8320]{2,1,0:T(1,128)}), f32[32,1,8320]{2,1,0:T(1,128)S(1)}, u32[]{:S(2)}, u32[]{:S(2)}) %all-to-all-start.7) | async-done | bytes 1064992 | tf_op jit(solution)/shard_map/all_to_all | solution.py:125
  431.2 3.8 copy.310
  436.1 3.3 fusion
  443.4 31.1 %reduce-scatter.7.cloned.1.call-done = f32[32,512]{1,0:T(8,128)} async-done(((f32[32,4096]{1,0:T(8,128)}), f32[32,512]{1,0:T(8,128)}) %reduce-scatter.7.cloned.1.call-update) | async-done | bytes 65552 | tf_op jit(solution)/shard_map/reduce_scatter | solution.py:140
  475.4 41.6 %reduce-scatter.9.cloned.1.call-done = f32[32,512]{1,0:T(8,128)} async-done(((f32[32,4096]{1,0:T(8,128)}), f32[32,512]{1,0:T(8,128)}) %reduce-scatter.9.cloned.1.call-update) | async-done | bytes 65552 | tf_op jit(solution)/shard_map/reduce_scatter | solution.py:140
  517.8 41.4 %reduce-scatter.11.cloned.1.call-done = f32[32,512]{1,0:T(8,128)} async-done(((f32[32,4096]{1,0:T(8,128)}), f32[32,512]{1,0:T(8,128)}) %reduce-scatter.11.cloned.1.call-update) | async-done | bytes 65552 | tf_op jit(solution)/shard_map/reduce_scatter | solution.py:140
  (367 shorter events, 91.2 us)
Async XLA Ops:
  7.2 376.9 %copy-start = (bf16[256,4096]{1,0:T(8,128)(2,1)S(1)}, bf16[256,4096]{1,0:T(8,128)(2,1)}, u32[]{:S(2)}) copy-start(bf16[256,4096]{1,0:T(8,128)(2,1)} %param.15) | copy-start | bytes 6291460
  12.2 35.4 %copy-start.54 = (f32[32,128]{1,0:T(8,128)}, f32[32,128]{1,0:T(8,128)S(1)}, u32[]{:S(2)}) copy-start(f32[32,128]{1,0:T(8,128)S(1)} %maximum_bitcast_fusion.4) | copy-start | bytes 49156
  12.3 35.3 %copy-start.67 = (f32[32,128]{1,0:T(8,128)}, f32[32,128]{1,0:T(8,128)S(1)}, u32[]{:S(2)}) copy-start(f32[32,128]{1,0:T(8,128)S(1)} %maximum_bitcast_fusion.5) | copy-start | bytes 49156
  45.2 138.7 %copy-start.24 = (f32[32,256]{1,0:T(8,128)}, f32[32,256]{1,0:T(8,128)S(1)}, u32[]{:S(2)}) copy-start(f32[32,256]{1,0:T(8,128)S(1)} %fusion.216) | copy-start | bytes 98308
  47.6 43.3 %copy-start.37 = (f32[32,2,64]{2,0,1:T(8,128)}, f32[32,2,64]{2,0,1:T(8,128)S(1)}, u32[]{:S(2)}) copy-start(f32[32,2,64]{2,0,1:T(8,128)S(1)} %get-tuple-element.118) | copy-start | bytes 49156
  47.6 45.4 %copy-start.35 = (f32[32,2,64]{2,0,1:T(8,128)}, f32[32,2,64]{2,0,1:T(8,128)S(1)}, u32[]{:S(2)}) copy-start(f32[32,2,64]{2,0,1:T(8,128)S(1)} %get-tuple-element.117) | copy-start | bytes 49156
  49.2 159.5 %all-to-all-start = ((bf16[32,32,2,128]{3,1,2,0:T(8,128)(2,1)}), bf16[32,32,2,128]{3,1,2,0:T(8,128)(2,1)}, u32[]{:S(2)}, u32[]{:S(2)}) async-start(bf16[32,32,2,128]{3,1,2,0:T(8,128)(2,1)} %stack.62), calls=%async_computation | async-start | bytes 1048576 | tf_op jit(solution)/shard_map/all_to_all | solution.py:75
  60.9 32.1 %copy-start.2 = (bf16[4096,256]{1,0:T(8,128)(2,1)S(1)}, bf16[4096,256]{1,0:T(8,128)(2,1)}, u32[]{:S(2)}) copy-start(bf16[4096,256]{1,0:T(8,128)(2,1)} %param.12) | copy-start | bytes 6291460
  93.0 76.2 %copy-start.21 = (f32[32,256]{1,0:T(8,128)}, f32[32,256]{1,0:T(8,128)S(1)}, u32[]{:S(2)}) copy-start(f32[32,256]{1,0:T(8,128)S(1)} %fusion.211) | copy-start | bytes 98308
  94.2 33.9 %copy-start.3 = (bf16[4096,256]{1,0:T(8,128)(2,1)S(1)}, bf16[4096,256]{1,0:T(8,128)(2,1)}, u32[]{:S(2)}) copy-start(bf16[4096,256]{1,0:T(8,128)(2,1)} %param.12) | copy-start | bytes 6291460
  125.8 3.4 copy-start.88
  125.8 32.4 %copy-start.1 = (bf16[4096,256]{1,0:T(8,128)(2,1)S(1)}, bf16[4096,256]{1,0:T(8,128)(2,1)}, u32[]{:S(2)}) copy-start(bf16[4096,256]{1,0:T(8,128)(2,1)} %param.13) | copy-start | bytes 6291460
  128.1 45.6 %copy-start.18 = (f32[32,256]{1,0:T(8,128)}, f32[32,256]{1,0:T(8,128)S(1)}, u32[]{:S(2)}) copy-start(f32[32,256]{1,0:T(8,128)S(1)} %fusion.206) | copy-start | bytes 98308
  158.3 6.9 %copy-start.26 = (bf16[4,256,256]{2,1,0:T(8,128)(2,1)S(1)}, bf16[4,256,256]{2,1,0:T(8,128)(2,1)}, u32[]{:S(2)}) copy-start(bf16[4,256,256]{2,1,0:T(8,128)(2,1)} %param.16) | copy-start | bytes 1572868
  158.8 19.5 %copy-start.16 = (f32[32,256]{1,0:T(8,128)}, f32[32,256]{1,0:T(8,128)S(1)}, u32[]{:S(2)}) copy-start(f32[32,256]{1,0:T(8,128)S(1)} %fusion.201) | copy-start | bytes 98308
  158.8 7.1 %copy-start.27 = (bf16[4,256,256]{2,1,0:T(8,128)(2,1)S(1)}, bf16[4,256,256]{2,1,0:T(8,128)(2,1)}, u32[]{:S(2)}) copy-start(bf16[4,256,256]{2,1,0:T(8,128)(2,1)} %param.17) | copy-start | bytes 1572868
  158.8 7.9 %copy-start.4 = (bf16[4096,256]{1,0:T(8,128)(2,1)S(1)}, bf16[4096,256]{1,0:T(8,128)(2,1)}, u32[]{:S(2)}) copy-start(bf16[4096,256]{1,0:T(8,128)(2,1)} %param.14) | copy-start | bytes 6291460
  158.8 7.9 %copy-start.93 = (f32[32]{0:T(128)S(1)}, f32[32]{0:T(128)}, u32[]{:S(2)}) copy-start(f32[32]{0:T(128)} %copy-done.92) | copy-start | bytes 388
  165.1 3.4 copy-start.79
  167.8 16.1 %copy-start.55 = (f32[32,128]{1,0:T(8,128)S(1)}, f32[32,128]{1,0:T(8,128)}, u32[]{:S(2)}) copy-start(f32[32,128]{1,0:T(8,128)} %copy-done.54) | copy-start | bytes 49156
  167.8 16.1 %copy-start.63 = (bf16[32,256]{1,0:T(8,128)(2,1)S(1)}, bf16[32,256]{1,0:T(8,128)(2,1)}, u32[]{:S(2)}) copy-start(bf16[32,256]{1,0:T(8,128)(2,1)} %convolution_convert_fusion.3) | copy-start | bytes 49156
  167.8 19.0 %copy-start.28 = (f32[32,256]{1,0:T(8,128)S(1)}, f32[32,256]{1,0:T(8,128)}, u32[]{:S(2)}) copy-start(f32[32,256]{1,0:T(8,128)} %fusion.213) | copy-start | bytes 98308
  167.8 20.4 %copy-start.29 = (f32[32,256]{1,0:T(8,128)S(1)}, f32[32,256]{1,0:T(8,128)}, u32[]{:S(2)}) copy-start(f32[32,256]{1,0:T(8,128)} %fusion.208) | copy-start | bytes 98308
  167.8 21.8 %copy-start.30 = (f32[32,256]{1,0:T(8,128)S(1)}, f32[32,256]{1,0:T(8,128)}, u32[]{:S(2)}) copy-start(f32[32,256]{1,0:T(8,128)} %fusion.203) | copy-start | bytes 98308
  172.2 19.9 %copy-start.49 = (f32[32,128]{1,0:T(8,128)}, f32[32,128]{1,0:T(8,128)S(1)}, u32[]{:S(2)}) copy-start(f32[32,128]{1,0:T(8,128)S(1)} %maximum_bitcast_fusion.8) | copy-start | bytes 49156
  176.8 15.4 %copy-start.47 = (f32[32,128]{1,0:T(8,128)}, f32[32,128]{1,0:T(8,128)S(1)}, u32[]{:S(2)}) copy-start(f32[32,128]{1,0:T(8,128)S(1)} %maximum_bitcast_fusion.10) | copy-start | bytes 49156
  180.7 11.5 %copy-start.43 = (f32[32,2,64]{2,0,1:T(8,128)}, f32[32,2,64]{2,0,1:T(8,128)S(1)}, u32[]{:S(2)}) copy-start(f32[32,2,64]{2,0,1:T(8,128)S(1)} %get-tuple-element.113) | copy-start | bytes 49156
  180.7 11.5 %copy-start.45 = (f32[32,2,64]{2,0,1:T(8,128)}, f32[32,2,64]{2,0,1:T(8,128)S(1)}, u32[]{:S(2)}) copy-start(f32[32,2,64]{2,0,1:T(8,128)S(1)} %get-tuple-element.114) | copy-start | bytes 49156
  182.2 9.9 %copy-start.41 = (f32[32,2,64]{2,0,1:T(8,128)}, f32[32,2,64]{2,0,1:T(8,128)S(1)}, u32[]{:S(2)}) copy-start(f32[32,2,64]{2,0,1:T(8,128)S(1)} %get-tuple-element.110) | copy-start | bytes 49156
  182.2 24.3 %copy-start.39 = (f32[32,2,64]{2,0,1:T(8,128)}, f32[32,2,64]{2,0,1:T(8,128)S(1)}, u32[]{:S(2)}) copy-start(f32[32,2,64]{2,0,1:T(8,128)S(1)} %get-tuple-element.109) | copy-start | bytes 49156
  183.8 22.7 %copy-start.31 = (f32[32,2,64]{2,0,1:T(8,128)}, f32[32,2,64]{2,0,1:T(8,128)S(1)}, u32[]{:S(2)}) copy-start(f32[32,2,64]{2,0,1:T(8,128)S(1)} %get-tuple-element.105) | copy-start | bytes 49156
  183.8 22.7 %copy-start.33 = (f32[32,2,64]{2,0,1:T(8,128)}, f32[32,2,64]{2,0,1:T(8,128)S(1)}, u32[]{:S(2)}) copy-start(f32[32,2,64]{2,0,1:T(8,128)S(1)} %get-tuple-element.106) | copy-start | bytes 49156
  186.8 36.0 %copy-start.15 = (pred[1024,32]{0,1:T(8,128)(4,1)}, pred[1024,32]{0,1:T(8,128)(4,1)S(1)}, u32[]{:S(2)}) copy-start(pred[1024,32]{0,1:T(8,128)(4,1)S(1)} %get-tuple-element.67) | copy-start | bytes 98308
  193.2 13.3 %copy-start.89 = (f32[32]{0:T(128)S(1)}, f32[32]{0:T(128)}, u32[]{:S(2)}) copy-start(f32[32]{0:T(128)} %copy-done.88) | copy-start | bytes 388
  202.4 4.1 copy-start.5
  203.8 3.8 copy-start.91
  207.6 13.3 %copy-start.25 = (f32[32,256]{1,0:T(8,128)S(1)}, f32[32,256]{1,0:T(8,128)}, u32[]{:S(2)}) copy-start(f32[32,256]{1,0:T(8,128)} %copy-done.24) | copy-start | bytes 98308
  207.6 13.4 %copy-start.36 = (f32[32,2,64]{2,0,1:T(8,128)S(1)}, f32[32,2,64]{2,0,1:T(8,128)}, u32[]{:S(2)}) copy-start(f32[32,2,64]{2,0,1:T(8,128)} %copy-done.35) | copy-start | bytes 49156
  207.6 13.4 %copy-start.38 = (f32[32,2,64]{2,0,1:T(8,128)S(1)}, f32[32,2,64]{2,0,1:T(8,128)}, u32[]{:S(2)}) copy-start(f32[32,2,64]{2,0,1:T(8,128)} %copy-done.37) | copy-start | bytes 49156
  207.6 13.4 %copy-start.56 = (f32[32,128]{1,0:T(8,128)S(1)}, f32[32,128]{1,0:T(8,128)}, u32[]{:S(2)}) copy-start(f32[32,128]{1,0:T(8,128)} %copy-done.54) | copy-start | bytes 49156
  207.7 13.4 %copy-start.68 = (f32[32,128]{1,0:T(8,128)S(1)}, f32[32,128]{1,0:T(8,128)}, u32[]{:S(2)}) copy-start(f32[32,128]{1,0:T(8,128)} %copy-done.67) | copy-start | bytes 49156
  208.8 12.6 %copy-start.95 = (pred[256]{0:T(512)(128)(4,1)S(1)}, pred[256]{0:T(512)(128)(4,1)}, u32[]{:S(2)}) copy-start(pred[256]{0:T(512)(128)(4,1)} %fusion.171) | copy-start | bytes 772
  209.7 27.2 %all-to-all-start.2 = ((bf16[32,32,2,128]{3,1,2,0:T(8,128)(2,1)}), bf16[32,32,2,128]{3,1,2,0:T(8,128)(2,1)}, u32[]{:S(2)}, u32[]{:S(2)}) async-start(bf16[32,32,2,128]{3,1,2,0:T(8,128)(2,1)} %stack.67), calls=%async_computation.3 | async-start | bytes 1048576 | tf_op jit(solution)/shard_map/all_to_all | solution.py:75
  227.9 9.0 %copy-start.81 = (bf16[32,2,128]{2,0,1:T(8,128)(2,1)S(1)}, bf16[32,2,128]{2,0,1:T(8,128)(2,1)}, u32[]{:S(2)}) copy-start(bf16[32,2,128]{2,0,1:T(8,128)(2,1)} %get-tuple-element.48) | copy-start | bytes 49156
  237.9 24.4 %all-to-all-start.4 = ((bf16[32,32,2,128]{3,1,2,0:T(8,128)(2,1)}), bf16[32,32,2,128]{3,1,2,0:T(8,128)(2,1)}, u32[]{:S(2)}, u32[]{:S(2)}) async-start(bf16[32,32,2,128]{3,1,2,0:T(8,128)(2,1)} %stack.72), calls=%async_computation.6 | async-start | bytes 1048576 | tf_op jit(solution)/shard_map/all_to_all | solution.py:75
  245.3 3.3 copy-start.14
  245.3 3.6 copy-start.11
  245.3 3.6 copy-start.94
  263.9 24.7 %all-to-all-start.6 = ((bf16[32,32,2,128]{3,1,2,0:T(8,128)(2,1)}), bf16[32,32,2,128]{3,1,2,0:T(8,128)(2,1)}, u32[]{:S(2)}, u32[]{:S(2)}) async-start(bf16[32,32,2,128]{3,1,2,0:T(8,128)(2,1)} %stack.77), calls=%async_computation.9 | async-start | bytes 1048576 | tf_op jit(solution)/shard_map/all_to_all | solution.py:75
  288.7 34.3 %all-to-all-start.1 = ((f32[32,1,8320]{2,1,0:T(1,128)}), f32[32,1,8320]{2,1,0:T(1,128)S(1)}, u32[]{:S(2)}, u32[]{:S(2)}) async-start(f32[32,1,8320]{2,1,0:T(1,128)} %copy.249), calls=%async_computation.1 | async-start | bytes 2129920 | tf_op jit(solution)/shard_map/all_to_all | solution.py:125
  296.8 3.6 copy-start.10
  296.8 3.6 copy-start.97
  323.0 35.1 %all-to-all-start.3 = ((f32[32,1,8320]{2,1,0:T(1,128)}), f32[32,1,8320]{2,1,0:T(1,128)}, u32[]{:S(2)}, u32[]{:S(2)}) async-start(f32[32,1,8320]{2,1,0:T(1,128)} %copy.269), calls=%async_computation.4 | async-start | bytes 2129920 | tf_op jit(solution)/shard_map/all_to_all | solution.py:125
  332.1 3.6 copy-start.96
  358.1 35.5 %all-to-all-start.5 = ((f32[32,1,8320]{2,1,0:T(1,128)}), f32[32,1,8320]{2,1,0:T(1,128)}, u32[]{:S(2)}, u32[]{:S(2)}) async-start(f32[32,1,8320]{2,1,0:T(1,128)} %copy.289), calls=%async_computation.7 | async-start | bytes 2129920 | tf_op jit(solution)/shard_map/all_to_all | solution.py:125
  365.5 77.0 %reduce-scatter.5.cloned.1.call-start = ((), (), s32[]{:S(2)}) async-start(), calls=%async_computation.12 | async-start | bytes 589824 | tf_op jit(solution)/shard_map/reduce_scatter | solution.py:140
  380.4 3.7 copy-start.86
  393.6 37.6 %all-to-all-start.7 = ((f32[32,1,8320]{2,1,0:T(1,128)}), f32[32,1,8320]{2,1,0:T(1,128)S(1)}, u32[]{:S(2)}, u32[]{:S(2)}) async-start(f32[32,1,8320]{2,1,0:T(1,128)} %copy.309), calls=%async_computation.10 | async-start | bytes 2129920 | tf_op jit(solution)/shard_map/all_to_all | solution.py:125
  403.4 71.1 %reduce-scatter.7.cloned.1.call-start = ((), (), s32[]{:S(2)}) async-start(), calls=%async_computation.13 | async-start | bytes 589824 | tf_op jit(solution)/shard_map/reduce_scatter | solution.py:140
  404.1 3.7 copy-start.85
  409.2 107.8 %reduce-scatter.9.cloned.1.call-start = ((), (), s32[]{:S(2)}) async-start(), calls=%async_computation.14 | async-start | bytes 589824 | tf_op jit(solution)/shard_map/reduce_scatter | solution.py:140
  415.6 3.7 copy-start.84
  420.7 138.6 %reduce-scatter.11.cloned.1.call-start = ((), (), s32[]{:S(2)}) async-start(), calls=%async_computation.15 | async-start | bytes 589824 | tf_op jit(solution)/shard_map/reduce_scatter | solution.py:140
  436.1 3.7 copy-start.83
  (46 other events, 105.2 us)
Sparse Core Ops, SparseCore 0:
  385.6 44.2 reduce-scatter.4
  432.3 42.1 reduce-scatter.6
  477.0 39.8 reduce-scatter.8
  519.3 39.8 reduce-scatter.10
